TPU v7x, 128 devices: a whole 4x4x4 slice. The times are simulated.
128 devices in a mesh: req: 16 (over z, x), tp: 8 (over y, core).
Axes of the slice: x: 4, y: 4, z: 4, core: 2. Of those that a mesh axis runs over, the one named last changes fastest.
Arguments:
- tokens: bfloat16 [8192, 3072], P('req', 'tp'), may hold values from -3 to 3
- norm_gain: bfloat16 [3072], P('tp'), may hold values from 0.099609375 to 1.8984375
- w_query: bfloat16 [3072, 3072], P(None, 'tp'), may hold values from -0.3125 to 0.3125
- w_key: bfloat16 [3072, 3072], P(None, 'tp'), may hold values from -0.109375 to 0.109375
- w_value: bfloat16 [3072, 3072], P(None, 'tp'), may hold values from -0.109375 to 0.109375
- w_out: bfloat16 [3072, 3072], P('tp'), may hold values from -0.109375 to 0.109375
- prev_keys: bfloat16 [65536, 3072], P('req', 'tp'), may hold values from -300 to 300
- prev_values: bfloat16 [65536, 3072], P('req', 'tp'), may hold values from -6 to 6
- earlier_lengths: int32 [16, 4], P('req'), may hold values from 1 to 2048, 4096 in all within a row
- new_lengths: int32 [16, 4], P('req'), may hold values from 1 to 256, 512 in all within a row
- page_table: int32 [16, 36], P('req'), may hold values from 0 to 575, as said below
Outputs:
- layer_out: bfloat16 [8192, 3072], P('req', 'tp')
- decode_pool: bfloat16 [288, 8, 128, 1536], P('req', 'tp')
Inputs may be any that keep to these rules, and one draw needn't show every extreme that they name: `page_table`: every value appears exactly once. Among the pages of one index of req, at most 2 share the same value // 18, and in every draw some destination receives exactly 2 of them.
All inputs are finite; a program needn't handle non-finite values.
Results may differ from a plain program's by a relative error of at most 0.0075.
Values may be sent and summed in bfloat16 or wider, within the bound.
No kernel may reach another device: no remote copies, remote signals or barrier semaphores. Data moves between devices by JAX's collectives and lax.ppermute only.
A program may use at most 256 MiB of HBM per device.

v0:
```python
import math
import jax
import jax.numpy as jnp
from jax import lax
from jax.sharding import PartitionSpec as P

HD = 96
HG = 4
PAGE = 128
EPSILON = 1e-05
THETA = 10000.0


def from_partner(value, axis, distance):
    mask = 2**distance
    pairs = [(source, source ^ mask) for source in range(lax.axis_size(axis))]
    return lax.ppermute(value, axis, pairs)


def rotate(values, positions, head_size):
    count = values.shape[0]
    half_size = head_size // 2
    shaped = values.reshape(count, -1, head_size)
    freqs = jnp.exp(-math.log(THETA) * 2.0 * jnp.arange(half_size, dtype=jnp.float32) / head_size)
    angles = positions.astype(jnp.float32)[:, None] * freqs[None, :]
    cosine = jnp.cos(angles)[:, None, :]
    sine = jnp.sin(angles)[:, None, :]
    first = shaped[:, :, :half_size]
    second = shaped[:, :, half_size:]
    turned = jnp.concatenate(
        [first * cosine - second * sine, second * cosine + first * sine], axis=2
    )
    return turned.reshape(count, -1)


def request_ids(lengths, count):
    ends = jnp.cumsum(lengths)
    row_index = jnp.arange(count, dtype=jnp.int32)
    return jnp.sum((row_index[:, None] >= ends[None, :]).astype(jnp.int32), axis=1)


def block_layout(earlier, fresh, count):
    owners = request_ids(fresh, count)
    starts = jnp.cumsum(fresh) - fresh
    onehot = (owners[:, None] == jnp.arange(fresh.shape[0], dtype=jnp.int32)[None, :]).astype(
        jnp.int32
    )
    first_row = jnp.sum(onehot * starts[None, :], axis=1)
    before = jnp.sum(onehot * earlier[None, :], axis=1)
    row_index = jnp.arange(count, dtype=jnp.int32)
    return (owners, before + row_index - first_row)


def visible(earlier, owners, prev_count, count):
    prev_owner = request_ids(earlier, prev_count)
    row_index = jnp.arange(count, dtype=jnp.int32)
    old_part = owners[:, None] == prev_owner[None, :]
    new_part = (owners[:, None] == owners[None, :]) & (row_index[None, :] <= row_index[:, None])
    return jnp.concatenate([old_part, new_part], axis=1)


def order_pair(mine, partner, own_half):
    lower = jnp.where(own_half == 0, mine, partner)
    upper = jnp.where(own_half == 0, partner, mine)
    return jnp.stack([lower, upper], axis=1)


def join_heads(stacked, local_width):
    count, halves, rows_page = (stacked.shape[0], stacked.shape[1], stacked.shape[2])
    split_rows = stacked.reshape(count, halves, rows_page, 2, local_width)
    return split_rows.transpose(0, 2, 3, 1, 4).reshape(count, rows_page, 2 * halves * local_width)


def fill_pool(page_rows, slot_ids, slot_count):
    empty = jnp.zeros((slot_count + 1, page_rows.shape[1], page_rows.shape[2]), jnp.bfloat16)
    return empty.at[slot_ids].set(page_rows)[:slot_count][:, None]


def shards(
    tokens,
    norm_gain,
    w_query,
    w_key,
    w_value,
    w_out,
    prev_keys,
    prev_values,
    earlier_lengths,
    new_lengths,
    page_table,
):
    token_count, local_width = tokens.shape
    full_width = w_query.shape[0]
    widened = tokens.astype(jnp.float32)
    square_sums = lax.psum(jnp.sum(widened * widened, axis=1), "tp")
    scaling = lax.rsqrt(square_sums / full_width + EPSILON)
    normed = (widened * scaling[:, None] * norm_gain.astype(jnp.float32)[None, :]).astype(
        jnp.bfloat16
    )
    fragment = lax.all_gather(normed, "tp", axis=1, tiled=True)
    query_raw, key_raw, value_raw = tuple(
        (
            jnp.dot(fragment, weight, preferred_element_type=jnp.float32)
            for weight in (w_query, w_key, w_value)
        )
    )
    earlier = earlier_lengths[0]
    fresh = new_lengths[0]
    owners, positions = block_layout(earlier, fresh, token_count)
    queries = rotate(query_raw, positions, HD).astype(jnp.bfloat16)
    new_keys = rotate(key_raw, positions, HD).astype(jnp.bfloat16)
    new_values = value_raw.astype(jnp.bfloat16)
    keys_all = jnp.concatenate([prev_keys, new_keys], axis=0)
    values_all = jnp.concatenate([prev_values, new_values], axis=0)
    allowed = visible(earlier, owners, prev_keys.shape[0], token_count)
    heads_here = local_width // HD
    scores = jnp.einsum(
        "qhd,khd->hqk",
        queries.reshape(token_count, heads_here, HD),
        keys_all.reshape(-1, heads_here, HD),
        preferred_element_type=jnp.float32,
    ) * HD ** (-0.5)
    scores = jnp.where(allowed[None, :, :], scores, -1e30)
    row_peak = jnp.max(scores, axis=2, keepdims=True)
    weights = jnp.exp(scores - row_peak)
    totals = jnp.sum(weights, axis=2)
    prob_rows = weights.astype(jnp.bfloat16)
    mixture = jnp.einsum(
        "hqk,khd->qhd",
        prob_rows,
        values_all.reshape(-1, heads_here, HD),
        preferred_element_type=jnp.float32,
    )
    attended = (
        (mixture / totals.T[:, :, None]).astype(jnp.bfloat16).reshape(token_count, local_width)
    )
    projected = jnp.dot(attended, w_out, preferred_element_type=jnp.float32)
    summed = lax.psum_scatter(projected, "tp", scatter_dimension=1, tiled=True)
    layer_out = (tokens.astype(jnp.float32) + summed).astype(jnp.bfloat16)
    page_total = keys_all.shape[0] // PAGE
    page_rows = jnp.concatenate(
        [
            keys_all.reshape(page_total, PAGE, local_width),
            values_all.reshape(page_total, PAGE, local_width),
        ],
        axis=2,
    )
    req_count = lax.axis_size("req")
    halves = lax.axis_size("tp") // HG
    slot_count = page_total // halves
    dest_count = req_count * halves
    capacity = 2 * ((page_total // 2 + dest_count - 1) // dest_count)
    table = page_table[0]
    target = table // slot_count
    slot_ids = table % slot_count
    own_half = lax.axis_index("tp") % halves
    order_index = jnp.arange(page_total, dtype=jnp.int32)
    earlier_mask = order_index[:, None] > order_index[None, :]
    placing = jnp.sum(
        ((target[:, None] == target[None, :]) & earlier_mask).astype(jnp.int32), axis=1
    )
    bucket = target * capacity + placing
    send_rows = (
        jnp.zeros((dest_count * capacity, PAGE, 2 * local_width), jnp.bfloat16)
        .at[bucket]
        .set(page_rows)
    )
    send_slots = jnp.full((dest_count * capacity,), slot_count, jnp.int32).at[bucket].set(slot_ids)
    got_rows, got_slots = (
        lax.all_to_all(send_rows, "req", split_axis=0, concat_axis=0, tiled=True),
        lax.all_to_all(send_slots, "req", split_axis=0, concat_axis=0, tiled=True),
    )
    got_rows = got_rows.reshape(req_count, halves, capacity, PAGE, 2 * local_width)
    got_slots = got_slots.reshape(req_count, halves, capacity)
    mine = lax.dynamic_index_in_dim(got_rows, own_half, 1, keepdims=False).reshape(
        req_count * capacity, PAGE, 2 * local_width
    )
    final_slots = lax.dynamic_index_in_dim(got_slots, own_half, 1, keepdims=False).reshape(-1)
    other = lax.dynamic_index_in_dim(got_rows, 1 - own_half, 1, keepdims=False).reshape(
        req_count * capacity, PAGE, 2 * local_width
    )
    partner = from_partner(other, "tp", 0)
    stacked = order_pair(mine, partner, own_half)
    final_rows = join_heads(stacked, local_width)
    decode_pool = fill_pool(final_rows, final_slots, slot_count)
    return (layer_out, decode_pool)


def solution(mesh):
    placed = (
        P("req", "tp"),
        P("tp"),
        P(None, "tp"),
        P(None, "tp"),
        P(None, "tp"),
        P("tp", None),
        P("req", "tp"),
        P("req", "tp"),
        P("req", None),
        P("req", None),
        P("req", None),
    )
    return jax.shard_map(
        shards,
        mesh=mesh,
        in_specs=placed,
        out_specs=(P("req", "tp"), P("req", "tp", None, None)),
        check_vma=False,
    )
```

profile of v0, /device:TPU:1, one launch (start us, length us, event | category | flops | bytes accessed | tf_op | source)
XLA Modules:
  0.0 441.5 jit_solution(15881802135246873474)
XLA Ops:
  9.2 13.5 %psum.7 = f32[512]{0:T(512)S(1)} all-reduce(f32[512]{0:T(512)S(1)} %fusion.16), channel_id=1, replica_groups=mesh['req'=16,'tp'=8] {'tp'}, use_global_device_ids=true, to_apply=%region_1.0 | all-reduce | flops 512 | bytes 4096 | tf_op jit(solution)/shard_map/psum | solution.py:95
  22.7 1.9 fusion.18
  32.0 1.6 pad_add_fusion
  33.6 21.3 %all-gather.2.cloned.1.call-done = bf16[512,3072]{1,0:T(8,128)(2,1)} async-done(((bf16[512,384]{1,0:T(8,128)(2,1)}), bf16[512,3072]{1,0:T(8,128)(2,1)}) %all-gather.2.cloned.1.call-update) | async-done | bytes 3145744 | tf_op jit(solution)/shard_map/all_gather | solution.py:100
  54.9 4.2 fusion.38
  59.2 1.4 fusion.37
  61.1 4.0 pad_maximum_fusion.2
  65.1 5.8 %copy.54 = bf16[4608,384]{0,1:T(8,128)(2,1)} copy(bf16[4608,384]{1,0:T(8,128)(2,1)} %pad_maximum_fusion.2) | data formatting | bytes 7077888 | tf_op jit(solution)/shard_map/concatenate | solution.py:113
  70.9 4.5 %convolution_convert_fusion = bf16[512,384]{1,0:T(8,128)(2,1)S(1)} fusion(bf16[512,3072]{1,0:T(8,128)(2,1)} %all-gather.2.cloned.1.call-done, bf16[3072,384]{1,0:T(8,128)(2,1)} %param.15), kind=kOutput, calls=%fused_computation.20 | convolution fusion | flops 1208156160 | bytes 5898240 | tf_op jit(solution)/shard_map/dot_general | solution.py:103
  75.8 7.1 %pad_maximum_fusion = bf16[36,128,768]{2,1,0:T(8,128)(2,1)} fusion(bf16[36,128,384]{2,1,0:T(8,128)(2,1)S(1)} %bitcast.89, bf16[36,128,384]{2,1,0:T(8,128)(2,1)} %bitcast.90), kind=kLoop, calls=%fused_computation.13 | loop fusion | flops 14155776 | bytes 14155776 | tf_op jit(solution)/shard_map/concatenate | solution.py:141
  82.9 6.0 %broadcast_in_dim.20 = bf16[64,128,768]{2,1,0:T(8,128)(2,1)} broadcast(bf16[]{:T(256)} %constant.76.clone.1), dimensions={} | broadcast | bytes 12582914 | tf_op jit(solution)/shard_map/broadcast_in_dim | solution.py:164
  88.9 22.5 %scatter_fusion = bf16[64,128,768]{2,1,0:T(8,128)(2,1)} fusion(bf16[64,128,768]{2,1,0:T(8,128)(2,1)} %broadcast_in_dim.20, s32[36]{0:T(128)S(1)} %fusion.29, bf16[36,128,768]{2,1,0:T(8,128)(2,1)} %pad_maximum_fusion), kind=kCustom, calls=%fused_computation.1 | custom fusion | bytes 21233808 | tf_op jit(solution)/shard_map/scatter | solution.py:166
  111.4 6.7 %all-to-all-start.1 = ((bf16[64,128,768]{2,1,0:T(8,128)(2,1)}), bf16[64,128,768]{2,1,0:T(8,128)(2,1)}, u32[]{:S(2)}, u32[]{:S(2)}) async-start(bf16[64,128,768]{2,1,0:T(8,128)(2,1)} %scatter_fusion), calls=%async_computation.2 | async-start | bytes 25165824 | tf_op jit(solution)/shard_map/all_to_all | solution.py:170
  118.3 18.6 %fusion = (f32[4,512]{1,0:T(4,128)S(1)}, f32[4,512,4608]{2,1,0:T(8,128)}) fusion(pred[512,4608]{1,0:T(8,128)(4,1)} %pad_add_fusion, bf16[4608,4,96]{0,2,1:T(8,128)(2,1)} %bitcast.94, bf16[512,4,48]{0,2,1:T(8,128)(2,1)S(1)} %get-tuple-element.17, bf16[512,4,48]{0,2,1:T(8,128)(2,1)S(1)} %get-tuple-element.16), kind=kOutput, calls=%fused_computation.5 | convolution fusion | flops 1841035264 | bytes 44048384 | tf_op jit(solution)/shard_map/qhd,khd->hqk/dot_general | solution.py:117
  136.8 5.7 %copy.52 = bf16[4608,384]{0,1:T(8,128)(2,1)} copy(bf16[4608,384]{1,0:T(8,128)(2,1)} %copy-done.1) | data formatting | bytes 7077888 | tf_op jit(solution)/shard_map/concatenate | solution.py:114
  142.6 18.2 %fusion.1 = f32[4,512]{1,0:T(4,128)S(1)} fusion(f32[4,512,4608]{2,1,0:T(8,128)} %get-tuple-element.26, f32[4,512]{1,0:T(4,128)S(1)} %get-tuple-element.25, pred[512,4608]{1,0:T(8,128)(4,1)} %pad_add_fusion), kind=kLoop, calls=%fused_computation.6 | loop fusion | flops 37746688 | bytes 40124416 | tf_op jit(solution)/shard_map/reduce_sum | solution.py:126
  160.8 15.3 %fusion.12 = bf16[512,4,96]{0,2,1:T(8,128)(2,1)S(1)} fusion(bf16[4608,4,96]{0,2,1:T(8,128)(2,1)S(1)} %bitcast.95, f32[4,512,4608]{2,1,0:T(8,128)} %get-tuple-element.26, f32[4,512]{1,0:T(4,128)S(1)} %get-tuple-element.25, pred[512,4608]{1,0:T(8,128)(4,1)S(1)} %copy-done.2, f32[512,4]{0,1:T(4,128)S(1)} %bitcast.100), kind=kOutput, calls=%fused_computation.25 | convolution fusion | flops 1850081280 | bytes 44056576 | tf_op jit(solution)/shard_map/hqk,khd->qhd/dot_general | solution.py:128
  176.2 4.5 %fusion.39 = f32[512,3072]{1,0:T(8,128)} fusion(bf16[512,384]{0,1:T(8,128)(2,1)S(1)} %bitcast.99, bf16[384,3072]{1,0:T(8,128)(2,1)S(1)} %copy-done), kind=kOutput, calls=%fused_computation.83 | convolution fusion | flops 1207959552 | bytes 9043968 | tf_op jit(solution)/shard_map/dot_general | solution.py:137
  180.7 125.3 %all-to-all-done.1 = bf16[64,128,768]{2,1,0:T(8,128)(2,1)} async-done(((bf16[64,128,768]{2,1,0:T(8,128)(2,1)}), bf16[64,128,768]{2,1,0:T(8,128)(2,1)}, u32[]{:S(2)}, u32[]{:S(2)}) %all-to-all-start.1) | async-done | bytes 12582944 | tf_op jit(solution)/shard_map/all_to_all | solution.py:170
  306.0 10.7 %constant_dynamic-slice_fusion = (bf16[16,1,2,128,768]{4,3,2,1,0:T(8,128)(2,1)}, bf16[16,1,2,128,768]{4,3,2,1,0:T(8,128)(2,1)}) fusion(bf16[16,2,2,128,768]{4,3,2,1,0:T(8,128)(2,1)} %bitcast.28, s32[]{:T(128)S(6)} %select_n.86, s32[]{:T(128)S(6)} %select_n.89), kind=kLoop, calls=%fused_computation.63 | loop fusion | bytes 25165832 | tf_op jit(solution)/shard_map/jit(dynamic_index_in_dim)/dynamic_slice | solution.py:175
  319.5 3.7 all-to-all-start
  323.2 6.0 %all-to-all-done = s32[16,4,1]{1,2,0:T(1,128)S(1)} async-done(((s32[16,4,1]{1,2,0:T(1,128)}), s32[16,4,1]{1,2,0:T(1,128)S(1)}, u32[]{:S(2)}, u32[]{:S(2)}) %all-to-all-start) | async-done | bytes 288 | tf_op jit(solution)/shard_map/all_to_all | solution.py:171
  329.5 2.0 fusion.19
  331.5 10.3 %bitcast_select_fusion.1 = (bf16[32,128,768]{2,1,0:T(8,128)(2,1)}, bf16[32,128,768]{2,1,0:T(8,128)(2,1)}) fusion(bf16[32,128,768]{2,1,0:T(8,128)(2,1)} %collective-permute-done, bf16[16,1,2,128,768]{4,3,2,1,0:T(8,128)(2,1)} %get-tuple-element.14, pred[]{:T(512)S(6)} %eq.75), kind=kLoop, calls=%fused_computation.15 | loop fusion | flops 6291456 | bytes 25165824 | tf_op jit(solution)/shard_map/jit(_where)/select_n | solution.py:63
  341.8 8.7 %copy.58 = bf16[32,128,768]{1,2,0:T(8,128)(2,1)} copy(bf16[32,128,768]{2,1,0:T(8,128)(2,1)} %get-tuple-element.12) | data formatting | bytes 12582912 | tf_op jit(solution)/shard_map/jit(_where)/select_n | solution.py:63
  350.5 8.6 %copy.59 = bf16[32,128,768]{1,2,0:T(8,128)(2,1)} copy(bf16[32,128,768]{2,1,0:T(8,128)(2,1)} %get-tuple-element.13) | data formatting | bytes 12582912 | tf_op jit(solution)/shard_map/jit(_where)/select_n | solution.py:64
  359.1 6.2 %maximum_bitcast_fusion = bf16[32,128,2,2,384]{1,4,2,0,3:T(8,128)(2,1)S(1)} fusion(bf16[32,1,128,2,384]{2,4,3,0,1:T(8,128)(2,1)} %bitcast.92, bf16[32,1,128,2,384]{2,4,3,0,1:T(8,128)(2,1)} %bitcast.91), kind=kLoop, calls=%fused_computation.10 | loop fusion | flops 6291456 | bytes 25165824 | tf_op jit(solution)/shard_map/transpose | solution.py:71
  365.3 5.7 %copy.60 = bf16[32,128,2,2,384]{1,4,3,2,0:T(8,128)(2,1)} copy(bf16[32,128,2,2,384]{1,4,2,0,3:T(8,128)(2,1)S(1)} %maximum_bitcast_fusion) | data formatting | bytes 25165824 | tf_op jit(solution)/shard_map/transpose | solution.py:71
  371.0 16.6 %copy.61 = bf16[32,128,1536]{2,1,0:T(8,128)(2,1)} copy(bf16[32,128,1536]{1,2,0:T(8,128)(2,1)} %bitcast.88) | data formatting | bytes 25165824 | tf_op jit(solution)/shard_map/reshape | solution.py:71
  387.6 3.7 broadcast_in_dim.18
  391.4 36.8 %scatter_fusion.1 = bf16[19,128,1536]{2,1,0:T(8,128)(2,1)} fusion(bf16[19,128,1536]{2,1,0:T(8,128)(2,1)} %broadcast_in_dim.18, s32[32]{0:T(128)S(1)} %fusion.30, bf16[32,128,1536]{2,1,0:T(8,128)(2,1)} %copy.61), kind=kCustom, calls=%fused_computation.2 | custom fusion | bytes 37748864 | tf_op jit(solution)/shard_map/scatter | solution.py:76
  428.1 6.6 %slice_bitcast_fusion = bf16[18,1,128,1536]{3,2,1,0:T(8,128)(2,1)} fusion(bf16[19,128,1536]{2,1,0:T(8,128)(2,1)} %scatter_fusion.1), kind=kLoop, calls=%fused_computation.12 | loop fusion | bytes 14155776
  (52 shorter events, 13.6 us)
Async XLA Ops:
  7.2 169.0 %copy-start = (bf16[384,3072]{1,0:T(8,128)(2,1)S(1)}, bf16[384,3072]{1,0:T(8,128)(2,1)}, u32[]{:S(2)}) copy-start(bf16[384,3072]{1,0:T(8,128)(2,1)} %param.16) | copy-start | bytes 7077892
  7.2 47.7 %all-gather.2.cloned.1.call-start = ((), (), s32[]{:S(2)}) async-start(), calls=%async_computation.3 | async-start | bytes 3538944 | tf_op jit(solution)/shard_map/all_gather | solution.py:100
  54.9 4.2 copy-start.6
  54.9 4.3 copy-start.7
  70.9 4.6 %copy-start.5 = (bf16[4096,384]{1,0:T(8,128)(2,1)S(1)}, bf16[4096,384]{1,0:T(8,128)(2,1)}, u32[]{:S(2)}) copy-start(bf16[4096,384]{1,0:T(8,128)(2,1)} %param.18) | copy-start | bytes 9437188
  75.8 7.1 %copy-start.1 = (bf16[4608,384]{1,0:T(8,128)(2,1)}, bf16[4608,384]{1,0:T(8,128)(2,1)S(1)}, u32[]{:S(2)}) copy-start(bf16[4608,384]{1,0:T(8,128)(2,1)S(1)} %pad_maximum_fusion.1) | copy-start | bytes 10616836
  111.4 194.7 %all-to-all-start.1 = ((bf16[64,128,768]{2,1,0:T(8,128)(2,1)}), bf16[64,128,768]{2,1,0:T(8,128)(2,1)}, u32[]{:S(2)}, u32[]{:S(2)}) async-start(bf16[64,128,768]{2,1,0:T(8,128)(2,1)} %scatter_fusion), calls=%async_computation.2 | async-start | bytes 25165824 | tf_op jit(solution)/shard_map/all_to_all | solution.py:170
  118.0 211.5 %reduce-scatter.2.cloned.1.call-start = ((), (), s32[]{:S(2)}) async-start(), calls=%async_computation.4 | async-start | bytes 7077888 | tf_op jit(solution)/shard_map/reduce_scatter | solution.py:138
  142.6 18.2 %copy-start.2 = (pred[512,4608]{1,0:T(8,128)(4,1)S(1)}, pred[512,4608]{1,0:T(8,128)(4,1)}, u32[]{:S(2)}) copy-start(pred[512,4608]{1,0:T(8,128)(4,1)} %pad_add_fusion) | copy-start | bytes 7077892
  142.6 18.2 %copy-start.3 = (bf16[4608,384]{0,1:T(8,128)(2,1)S(1)}, bf16[4608,384]{0,1:T(8,128)(2,1)}, u32[]{:S(2)}) copy-start(bf16[4608,384]{0,1:T(8,128)(2,1)} %copy.52) | copy-start | bytes 10616836
  306.0 23.5 %copy-start.4 = (bf16[512,384]{1,0:T(8,128)(2,1)S(1)}, bf16[512,384]{1,0:T(8,128)(2,1)}, u32[]{:S(2)}) copy-start(bf16[512,384]{1,0:T(8,128)(2,1)} %param.11) | copy-start | bytes 1179652
  316.7 14.8 %collective-permute-start = (bf16[32,128,768]{2,1,0:T(8,128)(2,1)}, bf16[32,128,768]{2,1,0:T(8,128)(2,1)}, u32[]{:S(2)}, u32[]{:S(2)}) collective-permute-start(bf16[32,128,768]{2,1,0:T(8,128)(2,1)} %bitcast.93), channel_id=1, source_target_pairs={{0,1},{1,0},{2,3},{3,2},{4,5},{5,4},{6,7},{7,6},{8,9},{9,8},{10,11... | collective-permute-start | bytes 18874376 | tf_op jit(solution)/shard_map/ppermute | solution.py:17
  319.5 9.7 %all-to-all-start = ((s32[16,4,1]{1,2,0:T(1,128)}), s32[16,4,1]{1,2,0:T(1,128)S(1)}, u32[]{:S(2)}, u32[]{:S(2)}) async-start(s32[16,4,1]{1,2,0:T(1,128)} %bitcast.23), calls=%async_computation.1 | async-start | bytes 16384 | tf_op jit(solution)/shard_map/all_to_all | solution.py:171
Sparse Core Ops, SparseCore 0:
  24.7 30.1 all-gather.1
  180.8 41.9 reduce-scatter.1
where the time goes:
time: 444 us; the launch traced here: 442 us
  waiting for transfers between devices  153 us (34%)
  local copies, waits for them, and re-layouts  139 us (31%)
  other arithmetic  61.3 us (14%)
  matrix products  48.6 us (11%)
  between operations  14.3 us (3%)
  blocking collectives  13.5 us (3%)
  starting transfers between devices  12 us (3%)
    all_to_all x1, waiting for transfers between devices, shards(): lax.all_to_all(send_rows, 'req', split_axis=0, concat_axis=0, tiled=True)  125 us
    scatter x1, local copies, waits for them, and re-layouts, fill_pool(): return empty.at[slot_ids].set(page_rows)[:slot_count][:, None]  36.8 us
    scatter x1, local copies, waits for them, and re-layouts, shards(): send_rows = jnp.zeros((dest_count * capacity, PAGE, 2 * local_width), jnp...  22.5 us
    all_gather x1, waiting for transfers between devices, shards(): fragment = lax.all_gather(normed, 'tp', axis=1, tiled=True)  21.3 us
    dot_general x1, matrix products, shards(): jnp.einsum('qhd,khd->hqk', queries.reshape(token_count, heads_here, HD),...  18.6 us
    reduce_sum x1, other arithmetic, shards(): totals = jnp.sum(weights, axis=2)  18.2 us
    reshape x1, local copies, waits for them, and re-layouts, join_heads(): split_rows.transpose(0, 2, 3, 1, 4)  16.6 us
    dot_general x1, matrix products, shards(): jnp.einsum('hqk,khd->qhd', prob_rows, values_all.reshape(-1, heads_here,...  15.3 us
  transfers between devices with their start and end apart: 5, of which 3 were waited for; matrix products, arithmetic and copies ran while one was open for 19% of the time, Pallas kernels for 0%

commit v1 on v0

--- a/solution.py
+++ b/solution.py
@@ -97,7 +97,9 @@
     normed = (widened * scaling[:, None] * norm_gain.astype(jnp.float32)[None, :]).astype(
         jnp.bfloat16
     )
-    fragment = lax.all_gather(normed, "tp", axis=1, tiled=True)
+    fragment = jnp.concatenate(
+        lax.all_to_all(jnp.stack([normed] * lax.axis_size("tp")), "tp", 0, 0), axis=1
+    )
     query_raw, key_raw, value_raw = tuple(
         (
             jnp.dot(fragment, weight, preferred_element_type=jnp.float32)

time: 444 us -> 474 us (1.068)
  local copies, waits for them, and re-layouts: 139 us -> 165 us
  starting transfers between devices: 12 us -> 22.1 us
  other arithmetic: 61.3 us -> 54.1 us
    all_to_all x0 -> x1, waiting for transfers between devices: none -> 24.6 us  [shards(): lax.all_to_all(jnp.stack([normed] * lax.axis_size('tp')), 'tp', 0, 0)]
    all_gather x1 -> x0, waiting for transfers between devices: 21.3 us -> none  [shards(): fragment = lax.all_gather(normed, 'tp', axis=1, tiled=True)]
    reshape x0 -> x3, local copies, waits for them, and re-layouts: none -> 15.5 us  [shards(): jnp.concatenate(lax.all_to_all(jnp.stack([normed] * lax.axis_size('tp')),...]
    unnamed x17 -> x27, local copies, waits for them, and re-layouts: 6.66 us -> 15.3 us
    all_to_all x0 -> x1, starting transfers between devices: none -> 7.23 us  [shards(): lax.all_to_all(jnp.stack([normed] * lax.axis_size('tp')), 'tp', 0, 0)]
where the time goes in v1:
time: 474 us; the launch traced here: 471 us
  local copies, waits for them, and re-layouts  165 us (35%)
  waiting for transfers between devices  153 us (32%)
  other arithmetic  54.1 us (11%)
  matrix products  48.6 us (10%)
  starting transfers between devices  22.1 us (5%)
  between operations  14.3 us (3%)
  blocking collectives  13.5 us (3%)
    all_to_all x1, waiting for transfers between devices, shards(): lax.all_to_all(send_rows, 'req', split_axis=0, concat_axis=0, tiled=True)  122 us
    scatter x1, local copies, waits for them, and re-layouts, fill_pool(): return empty.at[slot_ids].set(page_rows)[:slot_count][:, None]  36.8 us
    all_to_all x1, waiting for transfers between devices, shards(): lax.all_to_all(jnp.stack([normed] * lax.axis_size('tp')), 'tp', 0, 0)  24.6 us
    scatter x1, local copies, waits for them, and re-layouts, shards(): send_rows = jnp.zeros((dest_count * capacity, PAGE, 2 * local_width), jnp...  22.5 us
    dot_general x1, matrix products, shards(): jnp.einsum('qhd,khd->hqk', queries.reshape(token_count, heads_here, HD),...  18.6 us
    reduce_sum x1, other arithmetic, shards(): totals = jnp.sum(weights, axis=2)  18.2 us
    reshape x1, local copies, waits for them, and re-layouts, join_heads(): split_rows.transpose(0, 2, 3, 1, 4)  16.6 us
    reshape x3, local copies, waits for them, and re-layouts, shards(): jnp.concatenate(lax.all_to_all(jnp.stack([normed] * lax.axis_size('tp')),...  15.5 us
  transfers between devices with their start and end apart: 5, of which 3 were waited for; matrix products, arithmetic and copies ran while one was open for 19% of the time, Pallas kernels for 0%

profile of v1, /device:TPU:1, one launch (start us, length us, event | category | flops | bytes accessed | tf_op | source)
XLA Modules:
  0.0 471.1 jit_solution(8729467039895050697)
XLA Ops:
  9.2 13.5 %psum.7 = f32[512]{0:T(512)S(1)} all-reduce(f32[512]{0:T(512)S(1)} %fusion.16), channel_id=1, replica_groups=mesh['req'=16,'tp'=8] {'tp'}, use_global_device_ids=true, to_apply=%region_1.0 | all-reduce | flops 512 | bytes 4096 | tf_op jit(solution)/shard_map/psum | solution.py:95
  25.8 7.2 %all-to-all-start = ((bf16[8,512,384]{2,1,0:T(8,128)(2,1)}), bf16[8,512,384]{2,1,0:T(8,128)(2,1)}, u32[]{:S(2)}, u32[]{:S(2)}) async-start(bf16[8,512,384]{2,1,0:T(8,128)(2,1)} %stack.8), calls=%async_computation | async-start | bytes 6291456 | tf_op jit(solution)/shard_map/all_to_all | solution.py:101
  33.7 4.3 copy.65
  38.0 4.3 copy.66
  46.1 24.6 %all-to-all-done = bf16[8,512,384]{2,1,0:T(8,128)(2,1)} async-done(((bf16[8,512,384]{2,1,0:T(8,128)(2,1)}), bf16[8,512,384]{2,1,0:T(8,128)(2,1)}, u32[]{:S(2)}, u32[]{:S(2)}) %all-to-all-start) | async-done | bytes 3145760 | tf_op jit(solution)/shard_map/all_to_all | solution.py:101
  70.7 5.4 %copy.63 = bf16[512,8,384]{2,1,0:T(8,128)(2,1)} copy(bf16[512,8,384]{2,0,1:T(8,128)(2,1)} %bitcast) | data formatting | bytes 6291456 | tf_op jit(solution)/shard_map/reshape | solution.py:100
  76.1 5.8 %reshape.323 = bf16[512,3072,1]{1,0,2:T(8,128)(2,1)} reshape(bf16[512,8,384]{2,1,0:T(8,128)(2,1)} %copy.63) | data formatting | bytes 6291456 | tf_op jit(solution)/shard_map/reshape | solution.py:100
  81.9 4.2 fusion.38
  88.1 4.3 copy.77
  94.5 5.8 %copy.68 = bf16[4608,384]{0,1:T(8,128)(2,1)} copy(bf16[4608,384]{1,0:T(8,128)(2,1)} %pad_maximum_fusion.2) | data formatting | bytes 7077888 | tf_op jit(solution)/shard_map/concatenate | solution.py:115
  100.3 4.5 convolution_convert_fusion
  105.3 7.1 %pad_maximum_fusion = bf16[36,128,768]{2,1,0:T(8,128)(2,1)} fusion(bf16[36,128,384]{2,1,0:T(8,128)(2,1)S(1)} %bitcast.96, bf16[36,128,384]{2,1,0:T(8,128)(2,1)} %bitcast.97), kind=kLoop, calls=%fused_computation.13 | loop fusion | flops 14155776 | bytes 14155776 | tf_op jit(solution)/shard_map/concatenate | solution.py:143
  112.3 6.0 %broadcast_in_dim.20 = bf16[64,128,768]{2,1,0:T(8,128)(2,1)} broadcast(bf16[]{:T(256)} %constant.76.clone.1), dimensions={} | broadcast | bytes 12582914 | tf_op jit(solution)/shard_map/broadcast_in_dim | solution.py:166
  118.3 22.5 %scatter_fusion = bf16[64,128,768]{2,1,0:T(8,128)(2,1)} fusion(bf16[64,128,768]{2,1,0:T(8,128)(2,1)} %broadcast_in_dim.20, s32[36]{0:T(128)S(1)} %fusion.29, bf16[36,128,768]{2,1,0:T(8,128)(2,1)} %pad_maximum_fusion), kind=kCustom, calls=%fused_computation.1 | custom fusion | bytes 21233808 | tf_op jit(solution)/shard_map/scatter | solution.py:168
  140.8 7.6 %all-to-all-start.2 = ((bf16[64,128,768]{2,1,0:T(8,128)(2,1)}), bf16[64,128,768]{2,1,0:T(8,128)(2,1)}, u32[]{:S(2)}, u32[]{:S(2)}) async-start(bf16[64,128,768]{2,1,0:T(8,128)(2,1)} %scatter_fusion), calls=%async_computation.3 | async-start | bytes 25165824 | tf_op jit(solution)/shard_map/all_to_all | solution.py:172
  148.5 18.6 %fusion = (f32[4,512]{1,0:T(4,128)S(1)}, f32[4,512,4608]{2,1,0:T(8,128)}) fusion(pred[512,4608]{1,0:T(8,128)(4,1)} %pad_add_fusion, bf16[4608,4,96]{0,2,1:T(8,128)(2,1)} %bitcast.101, bf16[512,4,48]{0,2,1:T(8,128)(2,1)S(1)} %get-tuple-element.17, bf16[512,4,48]{0,2,1:T(8,128)(2,1)S(1)} %get-tuple-element.16), kind=kOutput, calls=%fused_computation.5 | convolution fusion | flops 1841035264 | bytes 44048384 | tf_op jit(solution)/shard_map/qhd,khd->hqk/dot_general | solution.py:119
  167.0 5.7 %copy.64 = bf16[4608,384]{0,1:T(8,128)(2,1)} copy(bf16[4608,384]{1,0:T(8,128)(2,1)} %copy-done.1) | data formatting | bytes 7077888 | tf_op jit(solution)/shard_map/concatenate | solution.py:116
  172.8 18.2 %fusion.1 = f32[4,512]{1,0:T(4,128)S(1)} fusion(f32[4,512,4608]{2,1,0:T(8,128)} %get-tuple-element.26, f32[4,512]{1,0:T(4,128)S(1)} %get-tuple-element.25, pred[512,4608]{1,0:T(8,128)(4,1)} %pad_add_fusion), kind=kLoop, calls=%fused_computation.6 | loop fusion | flops 37746688 | bytes 40124416 | tf_op jit(solution)/shard_map/reduce_sum | solution.py:128
  191.0 15.3 %fusion.12 = bf16[512,4,96]{0,2,1:T(8,128)(2,1)S(1)} fusion(bf16[4608,4,96]{0,2,1:T(8,128)(2,1)S(1)} %bitcast.102, f32[4,512,4608]{2,1,0:T(8,128)} %get-tuple-element.26, f32[4,512]{1,0:T(4,128)S(1)} %get-tuple-element.25, pred[512,4608]{1,0:T(8,128)(4,1)S(1)} %copy-done.2, f32[512,4]{0,1:T(4,128)S(1)} %bitcast.108), kind=kOutput, calls=%fused_computation.25 | convolution fusion | flops 1850081280 | bytes 44056576 | tf_op jit(solution)/shard_map/hqk,khd->qhd/dot_general | solution.py:130
  206.4 4.5 fusion.39
  210.9 122.2 %all-to-all-done.2 = bf16[64,128,768]{2,1,0:T(8,128)(2,1)} async-done(((bf16[64,128,768]{2,1,0:T(8,128)(2,1)}), bf16[64,128,768]{2,1,0:T(8,128)(2,1)}, u32[]{:S(2)}, u32[]{:S(2)}) %all-to-all-start.2) | async-done | bytes 12582944 | tf_op jit(solution)/shard_map/all_to_all | solution.py:172
  333.2 10.7 %constant_dynamic-slice_fusion = (bf16[16,1,2,128,768]{4,3,2,1,0:T(8,128)(2,1)}, bf16[16,1,2,128,768]{4,3,2,1,0:T(8,128)(2,1)}) fusion(bf16[16,2,2,128,768]{4,3,2,1,0:T(8,128)(2,1)} %bitcast.31, s32[]{:T(128)S(6)} %select_n.86, s32[]{:T(128)S(6)} %select_n.89), kind=kLoop, calls=%fused_computation.63 | loop fusion | bytes 25165832 | tf_op jit(solution)/shard_map/jit(dynamic_index_in_dim)/dynamic_slice | solution.py:177
  347.3 5.2 %all-to-all-start.1 = ((s32[16,4,1]{1,2,0:T(1,128)}), s32[16,4,1]{1,2,0:T(1,128)S(1)}, u32[]{:S(2)}, u32[]{:S(2)}) async-start(s32[16,4,1]{1,2,0:T(1,128)} %bitcast.26), calls=%async_computation.2 | async-start | bytes 16384 | tf_op jit(solution)/shard_map/all_to_all | solution.py:173
  352.5 6.3 %all-to-all-done.1 = s32[16,4,1]{1,2,0:T(1,128)S(1)} async-done(((s32[16,4,1]{1,2,0:T(1,128)}), s32[16,4,1]{1,2,0:T(1,128)S(1)}, u32[]{:S(2)}, u32[]{:S(2)}) %all-to-all-start.1) | async-done | bytes 288 | tf_op jit(solution)/shard_map/all_to_all | solution.py:173
  361.1 10.3 %bitcast_select_fusion.1 = (bf16[32,128,768]{2,1,0:T(8,128)(2,1)}, bf16[32,128,768]{2,1,0:T(8,128)(2,1)}) fusion(bf16[32,128,768]{2,1,0:T(8,128)(2,1)} %collective-permute-done, bf16[16,1,2,128,768]{4,3,2,1,0:T(8,128)(2,1)} %get-tuple-element.14, pred[]{:T(512)S(6)} %eq.75), kind=kLoop, calls=%fused_computation.15 | loop fusion | flops 6291456 | bytes 25165824 | tf_op jit(solution)/shard_map/jit(_where)/select_n | solution.py:63
  371.4 8.7 %copy.72 = bf16[32,128,768]{1,2,0:T(8,128)(2,1)} copy(bf16[32,128,768]{2,1,0:T(8,128)(2,1)} %get-tuple-element.12) | data formatting | bytes 12582912 | tf_op jit(solution)/shard_map/jit(_where)/select_n | solution.py:63
  380.1 8.6 %copy.73 = bf16[32,128,768]{1,2,0:T(8,128)(2,1)} copy(bf16[32,128,768]{2,1,0:T(8,128)(2,1)} %get-tuple-element.13) | data formatting | bytes 12582912 | tf_op jit(solution)/shard_map/jit(_where)/select_n | solution.py:64
  388.7 6.2 %maximum_bitcast_fusion = bf16[32,128,2,2,384]{1,4,2,0,3:T(8,128)(2,1)S(1)} fusion(bf16[32,1,128,2,384]{2,4,3,0,1:T(8,128)(2,1)} %bitcast.99, bf16[32,1,128,2,384]{2,4,3,0,1:T(8,128)(2,1)} %bitcast.98), kind=kLoop, calls=%fused_computation.10 | loop fusion | flops 6291456 | bytes 25165824 | tf_op jit(solution)/shard_map/transpose | solution.py:71
  394.8 5.7 %copy.74 = bf16[32,128,2,2,384]{1,4,3,2,0:T(8,128)(2,1)} copy(bf16[32,128,2,2,384]{1,4,2,0,3:T(8,128)(2,1)S(1)} %maximum_bitcast_fusion) | data formatting | bytes 25165824 | tf_op jit(solution)/shard_map/transpose | solution.py:71
  400.6 16.6 %copy.75 = bf16[32,128,1536]{2,1,0:T(8,128)(2,1)} copy(bf16[32,128,1536]{1,2,0:T(8,128)(2,1)} %bitcast.95) | data formatting | bytes 25165824 | tf_op jit(solution)/shard_map/reshape | solution.py:71
  420.9 36.8 %scatter_fusion.1 = bf16[19,128,1536]{2,1,0:T(8,128)(2,1)} fusion(bf16[19,128,1536]{2,1,0:T(8,128)(2,1)} %broadcast_in_dim.18, s32[32]{0:T(128)S(1)} %fusion.30, bf16[32,128,1536]{2,1,0:T(8,128)(2,1)} %copy.75), kind=kCustom, calls=%fused_computation.2 | custom fusion | bytes 37748864 | tf_op jit(solution)/shard_map/scatter | solution.py:76
  457.7 6.6 %slice_bitcast_fusion = bf16[18,1,128,1536]{3,2,1,0:T(8,128)(2,1)} fusion(bf16[19,128,1536]{2,1,0:T(8,128)(2,1)} %scatter_fusion.1), kind=kLoop, calls=%fused_computation.12 | loop fusion | bytes 14155776
  (65 shorter events, 23.4 us)
Async XLA Ops:
  7.2 199.2 %copy-start = (bf16[384,3072]{1,0:T(8,128)(2,1)S(1)}, bf16[384,3072]{1,0:T(8,128)(2,1)}, u32[]{:S(2)}) copy-start(bf16[384,3072]{1,0:T(8,128)(2,1)} %param.16) | copy-start | bytes 7077892
  7.2 25.8 %copy-start.11 = (s32[1,4]{1,0:T(1,128)S(1)}, s32[1,4]{1,0:T(1,128)}, u32[]{:S(2)}) copy-start(s32[1,4]{1,0:T(1,128)} %param.20) | copy-start | bytes 52
  7.2 26.0 %copy-start.9 = (s32[1,36]{1,0:T(1,128)S(1)}, s32[1,36]{1,0:T(1,128)}, u32[]{:S(2)}) copy-start(s32[1,36]{1,0:T(1,128)} %param.21) | copy-start | bytes 436
  7.2 26.3 %copy-start.10 = (s32[1,4]{1,0:T(1,128)S(1)}, s32[1,4]{1,0:T(1,128)}, u32[]{:S(2)}) copy-start(s32[1,4]{1,0:T(1,128)} %param.19) | copy-start | bytes 52
  25.8 44.9 %all-to-all-start = ((bf16[8,512,384]{2,1,0:T(8,128)(2,1)}), bf16[8,512,384]{2,1,0:T(8,128)(2,1)}, u32[]{:S(2)}, u32[]{:S(2)}) async-start(bf16[8,512,384]{2,1,0:T(8,128)(2,1)} %stack.8), calls=%async_computation | async-start | bytes 6291456 | tf_op jit(solution)/shard_map/all_to_all | solution.py:101
  81.9 4.2 copy-start.7
  81.9 4.3 copy-start.8
  88.1 4.3 copy-start.5
  100.3 4.6 copy-start.6
  105.2 7.1 %copy-start.1 = (bf16[4608,384]{1,0:T(8,128)(2,1)}, bf16[4608,384]{1,0:T(8,128)(2,1)S(1)}, u32[]{:S(2)}) copy-start(bf16[4608,384]{1,0:T(8,128)(2,1)S(1)} %pad_maximum_fusion.1) | copy-start | bytes 10616836
  140.8 192.4 %all-to-all-start.2 = ((bf16[64,128,768]{2,1,0:T(8,128)(2,1)}), bf16[64,128,768]{2,1,0:T(8,128)(2,1)}, u32[]{:S(2)}, u32[]{:S(2)}) async-start(bf16[64,128,768]{2,1,0:T(8,128)(2,1)} %scatter_fusion), calls=%async_computation.3 | async-start | bytes 25165824 | tf_op jit(solution)/shard_map/all_to_all | solution.py:172
  148.4 210.7 %reduce-scatter.2.cloned.1.call-start = ((), (), s32[]{:S(2)}) async-start(), calls=%async_computation.4 | async-start | bytes 7077888 | tf_op jit(solution)/shard_map/reduce_scatter | solution.py:140
  172.8 18.2 %copy-start.2 = (pred[512,4608]{1,0:T(8,128)(4,1)S(1)}, pred[512,4608]{1,0:T(8,128)(4,1)}, u32[]{:S(2)}) copy-start(pred[512,4608]{1,0:T(8,128)(4,1)} %pad_add_fusion) | copy-start | bytes 7077892
  172.8 18.2 %copy-start.3 = (bf16[4608,384]{0,1:T(8,128)(2,1)S(1)}, bf16[4608,384]{0,1:T(8,128)(2,1)}, u32[]{:S(2)}) copy-start(bf16[4608,384]{0,1:T(8,128)(2,1)} %copy.64) | copy-start | bytes 10616836
  333.2 25.9 %copy-start.4 = (bf16[512,384]{1,0:T(8,128)(2,1)S(1)}, bf16[512,384]{1,0:T(8,128)(2,1)}, u32[]{:S(2)}) copy-start(bf16[512,384]{1,0:T(8,128)(2,1)} %param.11) | copy-start | bytes 1179652
  343.9 17.2 %collective-permute-start = (bf16[32,128,768]{2,1,0:T(8,128)(2,1)}, bf16[32,128,768]{2,1,0:T(8,128)(2,1)}, u32[]{:S(2)}, u32[]{:S(2)}) collective-permute-start(bf16[32,128,768]{2,1,0:T(8,128)(2,1)} %bitcast.100), channel_id=1, source_target_pairs={{0,1},{1,0},{2,3},{3,2},{4,5},{5,4},{6,7},{7,6},{8,9},{9,8},{10,11... | collective-permute-start | bytes 18874376 | tf_op jit(solution)/shard_map/ppermute | solution.py:17
  347.3 11.5 %all-to-all-start.1 = ((s32[16,4,1]{1,2,0:T(1,128)}), s32[16,4,1]{1,2,0:T(1,128)S(1)}, u32[]{:S(2)}, u32[]{:S(2)}) async-start(s32[16,4,1]{1,2,0:T(1,128)} %bitcast.26), calls=%async_computation.2 | async-start | bytes 16384 | tf_op jit(solution)/shard_map/all_to_all | solution.py:173
Sparse Core Ops, SparseCore 0:
  211.0 41.9 reduce-scatter.1
